TPU v7x, 32 devices: a whole 2x2x4 slice. The times are simulated.
32 devices in a mesh: dp: 4 (over z), expert: 8 (over y, x, core).
Axes of the slice: x: 2, y: 2, z: 4, core: 2. Of those that a mesh axis runs over, the one named last changes fastest.
Arguments:
- hidden: bfloat16 [3072, 2880], P('expert', 'dp'), may hold values from -6 to 6
- segments: int32 [8, 384], P('expert'), may hold values from 0 to 3, never falling along the last dimension, each value on 1 to 192 neighbouring positions
- request_adapter: int32 [8, 4], P('expert'), may hold values from 0 to 7
- routes: int32 [8, 384, 4], P('expert', 'dp'), may hold values from 0 to 7, all different within a row; in each aligned block of 96 rows (0 to 95, 96 to 191, ..., all dimensions but the last counted through in order) at most 64 rows name the same one
- expert_gates: bfloat16 [8, 384, 4], P('expert', 'dp'), may hold values from 0.049804688 to 0.59765625
- attention_gain: float32 [2880], replicated, may hold values from 0.25 to 1.75
- joined_weight: bfloat16 [2880, 4, 640], P(None, 'dp'), may hold values from -0.109375 to 0.109375
- sinks: float32 [32], P('dp'), may hold values from 0 to 3
- attention_out_weight: bfloat16 [2048, 2880], P('dp'), may hold values from -0.125 to 0.125
- joined_down_maps: bfloat16 [2880, 128], replicated, may hold values from -0.109375 to 0.109375
- joined_up_maps: bfloat16 [128, 4, 640], P(None, 'dp'), may hold values from -0.375 to 0.375
- output_down_maps: bfloat16 [2048, 128], P('dp'), may hold values from -0.125 to 0.125
- output_up_maps: bfloat16 [128, 2880], P(None, 'dp'), may hold values from -0.75 to 0.75
- expert_norm_gain: float32 [2880], replicated, may hold values from 0.25 to 1.75
- expert_gate_weight: bfloat16 [8, 2880, 2880], P('expert', None, 'dp'), may hold values from -0.109375 to 0.109375
- expert_up_weight: bfloat16 [8, 2880, 2880], P('expert', None, 'dp'), may hold values from -0.109375 to 0.109375
- expert_down_weight: bfloat16 [8, 2880, 2880], P('expert', 'dp'), may hold values from -0.109375 to 0.109375
- closing_gain: float32 [2880], replicated, may hold values from 0.25 to 1.75
- vocabulary_weight: bfloat16 [2880, 25600], P(None, ('dp', 'expert')), may hold values from -0.109375 to 0.109375
Outputs:
- hidden_out: bfloat16 [3072, 2880], P('expert', 'dp')
- logits: float32 [32, 25600], P(None, ('dp', 'expert'))
Inputs may be any that keep to these rules, and one draw needn't show every extreme that they name: `segments`: in each column the ids do not fall; each of the 4 requests has 1 to 192 tokens, and one has exactly 192. `routes`: the 4 experts of a token differ. Within the rows of one device (96 consecutive tokens, aligned blocks) no expert is named more than 64 times, and in some blocks one expert is named exactly 64 times.
All inputs are finite; a program needn't handle non-finite values.
Results may differ from a plain program's by a relative error of at most 0.02.
Values may be sent and summed in bfloat16 or wider, within the bound.
No kernel may reach another device: no remote copies, remote signals or barrier semaphores. Data moves between devices by JAX's collectives and lax.ppermute only.
A program may use at most 128 MiB of HBM per device.

v0:
```python
import jax
import jax.numpy as jnp
from jax import lax
from jax.sharding import PartitionSpec as P

HEAD_SIZE = 64
QUERY_GROUP = 8
TOP = 4
ADAPTER_RANK = 16
REQS = 4
epsilon = 1e-05
theta_base = 150000.0
adapter_scale = 2.0
glu_alpha = 1.702


def rms_scale(values, gain_row):
    mean_square = jnp.mean(values * values, axis=-1, keepdims=True)
    return values * lax.rsqrt(mean_square + epsilon) * gain_row


def positions_of(segment_row):
    counter = jnp.arange(segment_row.shape[0], dtype=jnp.int32)
    starting = jnp.concatenate(
        [jnp.ones((1,), dtype=jnp.bool_), segment_row[1:] != segment_row[:-1]]
    )
    first_index = lax.cummax(jnp.where(starting, counter, 0), axis=0)
    return counter - first_index


def adapter_per_token(segment_row, adapter_row):
    hits = segment_row[:, None] == jnp.arange(adapter_row.shape[0], dtype=jnp.int32)[None, :]
    return jnp.sum(jnp.where(hits, adapter_row[None, :], 0), axis=1)


def rotate_heads(values, positions):
    head_dim = values.shape[-1]
    half_dim = head_dim // 2
    frequency = theta_base ** (-2.0 * jnp.arange(half_dim, dtype=jnp.float32) / head_dim)
    angles = positions.astype(jnp.float32)[:, None] * frequency[None, :]
    cosine = jnp.cos(angles)[:, None, :]
    sine_part = jnp.sin(angles)[:, None, :]
    first_half = values[..., :half_dim]
    second_half = values[..., half_dim:]
    return jnp.concatenate(
        [
            first_half * cosine - second_half * sine_part,
            second_half * cosine + first_half * sine_part,
        ],
        axis=-1,
    )


def attend_heads(queries, key_heads, value_heads, segment_row, sink_row):
    tokens_now, kv_now, group_now, head_dim = queries.shape
    scores = jnp.einsum(
        "tkgh,skh->kgts", queries, key_heads, preferred_element_type=jnp.float32
    ) * head_dim ** (-0.5)
    counter = jnp.arange(tokens_now, dtype=jnp.int32)
    allowed = (segment_row[:, None] == segment_row[None, :]) & (
        counter[None, :] <= counter[:, None]
    )
    weights = jnp.where(allowed[None, None], jnp.exp(scores), 0.0)
    totals = jnp.sum(weights, axis=-1, keepdims=True) + jnp.exp(sink_row).reshape(
        kv_now, group_now, 1, 1
    )
    probs = (weights / totals).astype(jnp.bfloat16)
    blended_hidden = jnp.einsum(
        "kgts,skh->tkgh", probs, value_heads, preferred_element_type=jnp.float32
    )
    return blended_hidden.astype(jnp.bfloat16).reshape(tokens_now, kv_now * group_now * head_dim)


def shards(
    hidden,
    segments,
    request_adapter,
    routes,
    expert_gates,
    attention_gain,
    joined_weight,
    sinks,
    attention_out_weight,
    joined_down_maps,
    joined_up_maps,
    output_down_maps,
    output_up_maps,
    expert_norm_gain,
    expert_gate_weight,
    expert_up_weight,
    expert_down_weight,
    closing_gain,
    vocabulary_weight,
):
    groups = lax.axis_size("dp")
    columns = lax.axis_size("expert")
    position_dp = lax.axis_index("dp")
    segment_row = segments[0]
    adapter_row = request_adapter[0]
    col_tokens = segment_row.shape[0]
    gathered_rows = lax.all_gather(hidden, "dp", axis=1, tiled=True)
    width = gathered_rows.shape[1]
    normalized_hidden = rms_scale(gathered_rows.astype(jnp.float32), attention_gain).astype(
        jnp.bfloat16
    )
    joined_projection = jnp.dot(
        normalized_hidden, joined_weight.reshape(width, -1), preferred_element_type=jnp.float32
    )
    reduced_every_adapter = joined_down_maps.shape[1]
    reduced_hidden = jnp.dot(
        normalized_hidden, joined_down_maps, preferred_element_type=jnp.float32
    ).astype(jnp.bfloat16)
    rank_owner = jnp.arange(reduced_every_adapter, dtype=jnp.int32) // ADAPTER_RANK
    adapter_mask = adapter_per_token(segment_row, adapter_row)[:, None] == rank_owner[None, :]
    selected_reduced = jnp.where(adapter_mask, reduced_hidden, jnp.zeros_like(reduced_hidden))
    joined_projection = joined_projection + adapter_scale * jnp.dot(
        selected_reduced,
        joined_up_maps.reshape(reduced_every_adapter, -1),
        preferred_element_type=jnp.float32,
    )
    kv_here = joined_weight.shape[1]
    joined_projection = joined_projection.reshape(col_tokens, kv_here, QUERY_GROUP + 2, HEAD_SIZE)
    positions = positions_of(segment_row)
    queries = rotate_heads(
        joined_projection[:, :, :QUERY_GROUP].reshape(col_tokens, kv_here * QUERY_GROUP, HEAD_SIZE),
        positions,
    )
    queries = queries.astype(jnp.bfloat16).reshape(col_tokens, kv_here, QUERY_GROUP, HEAD_SIZE)
    key_heads = rotate_heads(joined_projection[:, :, QUERY_GROUP], positions).astype(jnp.bfloat16)
    value_heads = joined_projection[:, :, QUERY_GROUP + 1].astype(jnp.bfloat16)
    blended_hidden = attend_heads(queries, key_heads, value_heads, segment_row, sinks)
    partial_out = jnp.dot(blended_hidden, attention_out_weight, preferred_element_type=jnp.float32)
    mine_out = lax.psum_scatter(
        partial_out.astype(jnp.bfloat16), "dp", scatter_dimension=1, tiled=True
    ).astype(jnp.float32)
    output_reduced = lax.psum(
        jnp.dot(blended_hidden, output_down_maps, preferred_element_type=jnp.float32).astype(
            jnp.bfloat16
        ),
        "dp",
    )
    selected_output = jnp.where(adapter_mask, output_reduced, jnp.zeros_like(output_reduced))
    adapter_delta = adapter_scale * jnp.dot(
        selected_output, output_up_maps, preferred_element_type=jnp.float32
    )
    resid = (hidden.astype(jnp.float32) + mine_out + adapter_delta).astype(jnp.bfloat16)
    column_full = lax.all_gather(resid, "dp", axis=1, tiled=True)
    moe_in = rms_scale(column_full.astype(jnp.float32), expert_norm_gain).astype(jnp.bfloat16)
    share = col_tokens // groups
    experts = expert_gate_weight.shape[0] * columns
    capacity = 4 * share * TOP // (3 * experts)
    col_capacity = groups * capacity
    route_col = lax.all_gather(routes[0], "dp", axis=0, tiled=True)
    gates_col = lax.all_gather(expert_gates[0], "dp", axis=0, tiled=True)
    route_flat = route_col.reshape(-1)
    one_hot = (route_flat[:, None] == jnp.arange(experts, dtype=jnp.int32)[None, :]).astype(
        jnp.int32
    )
    slot_rows = jnp.sum((jnp.cumsum(one_hot, axis=0) - one_hot) * one_hot, axis=1)
    target = route_flat * col_capacity + slot_rows
    source_rows = jnp.arange(route_flat.shape[0], dtype=jnp.int32) // TOP
    table = jnp.full((experts * col_capacity,), col_tokens, jnp.int32).at[target].set(source_rows)
    padded = jnp.concatenate([moe_in, jnp.zeros((1, width), jnp.bfloat16)], axis=0)
    outgoing = jnp.take(padded, table, axis=0).reshape(experts, col_capacity, width)
    gate_weight = expert_gate_weight[0]
    up_weight = expert_up_weight[0]
    down_weight = expert_down_weight[0]
    arrived = lax.all_to_all(outgoing, "expert", split_axis=0, concat_axis=0, tiled=True)
    rows_in = arrived.reshape(-1, width)
    gate_part = jnp.dot(rows_in, gate_weight, preferred_element_type=jnp.float32)
    up_part = jnp.dot(rows_in, up_weight, preferred_element_type=jnp.float32)
    activated = (gate_part * jax.nn.sigmoid(glu_alpha * gate_part) * (up_part + 1.0)).astype(
        jnp.bfloat16
    )
    shares_out = (
        jnp.dot(activated, down_weight, preferred_element_type=jnp.float32)
        .astype(jnp.bfloat16)
        .reshape(experts, col_capacity, width)
    )
    answers = lax.all_to_all(shares_out, "expert", split_axis=0, concat_axis=0, tiled=True)
    picked_out = jnp.take(answers.reshape(experts * col_capacity, width), target, axis=0).reshape(
        col_tokens, TOP, width
    )
    mixture = jnp.einsum("tk,tkd->td", gates_col, picked_out, preferred_element_type=jnp.float32)
    moe_part = lax.psum_scatter(mixture.astype(jnp.bfloat16), "dp", scatter_dimension=1, tiled=True)
    moe_rounded = moe_part.astype(jnp.float32).astype(jnp.bfloat16)
    hidden_out = (resid.astype(jnp.float32) + moe_rounded.astype(jnp.float32)).astype(jnp.bfloat16)
    counter = jnp.arange(col_tokens, dtype=jnp.int32)
    request_ids = jnp.arange(REQS, dtype=jnp.int32)
    last_index = jnp.max(
        jnp.where(segment_row[None, :] == request_ids[:, None], counter[None, :], -1), axis=1
    )
    chosen = jnp.take(hidden_out, jnp.clip(last_index, 0, col_tokens - 1), axis=0)
    spread_rows = lax.all_gather(chosen, ("dp", "expert"), axis=0, tiled=True)
    quarter = chosen.shape[1]
    tail_full = (
        spread_rows.reshape(groups, columns * REQS, quarter)
        .transpose(1, 0, 2)
        .reshape(columns * REQS, groups * quarter)
    )
    tail_rows = rms_scale(tail_full.astype(jnp.float32), closing_gain).astype(jnp.bfloat16)
    logits = jnp.dot(tail_rows, vocabulary_weight, preferred_element_type=jnp.float32)
    return (hidden_out, logits)


def solution(mesh):
    in_specs = (
        P("expert", "dp"),
        P("expert", None),
        P("expert", None),
        P("expert", "dp", None),
        P("expert", "dp", None),
        P(),
        P(None, "dp", None),
        P("dp"),
        P("dp", None),
        P(),
        P(None, "dp", None),
        P("dp", None),
        P(None, "dp"),
        P(),
        P("expert", None, "dp"),
        P("expert", None, "dp"),
        P("expert", "dp", None),
        P(),
        P(None, ("dp", "expert")),
    )
    out_specs = (P("expert", "dp"), P(None, ("dp", "expert")))
    return jax.shard_map(shards, mesh=mesh, in_specs=in_specs, out_specs=out_specs, check_vma=False)
```

profile of v0, /device:TPU:0, one launch (start us, length us, event | category | flops | bytes accessed | tf_op | source)
XLA Modules:
  0.0 773.1 jit_solution(7064949755682146424)
XLA Ops:
  7.2 0.7 all-gather.6.cloned.1.call-update
  8.0 0.8 reduce.7
  8.8 0.8 compare_reduce_fusion
  9.7 0.3 reduce-window.15
  10.1 0.7 exp.18
  10.9 0.9 select_reduce_fusion
  11.9 0.3 multiply_cosine_fusion
  12.3 48.1 %all-gather.6.cloned.1.call-done = bf16[384,2880]{0,1:T(8,128)(2,1)} async-done(((bf16[384,720]{0,1:T(8,128)(2,1)}), bf16[384,2880]{0,1:T(8,128)(2,1)}) %all-gather.6.cloned.1.call-update) | async-done | bytes 2211856 | tf_op jit(solution)/shard_map/all_gather | solution.py:101
  60.4 2.2 fusion
  62.6 5.9 fusion.14
  68.5 4.8 fusion.21
  73.3 2.5 copy.58
  75.8 1.2 slice_bitcast_fusion
  77.0 0.9 slice_bitcast_fusion.1
  77.9 0.3 fusion.63
  78.3 1.3 fusion.13
  79.6 2.3 fusion.23
  81.9 0.7 copy-done.4
  82.6 1.0 convolution_convert_fusion.2
  83.7 4.1 convolution_convert_fusion.1
  87.9 29.0 %all-reduce.3.cloned.1.call-done = bf16[384,128]{1,0:T(8,128)(2,1)} async-done(((bf16[384,128]{1,0:T(8,128)(2,1)}), bf16[384,128]{1,0:T(8,128)(2,1)}) %all-reduce.3.cloned.1.call-update) | async-done | bytes 98320 | tf_op jit(solution)/shard_map/psum | solution.py:136
  116.8 48.0 %reduce-scatter.3.cloned.1.call-done = bf16[384,720]{0,1:T(8,128)(2,1)} async-done(((bf16[384,2880]{0,1:T(8,128)(2,1)}), bf16[384,720]{0,1:T(8,128)(2,1)}) %reduce-scatter.3.cloned.1.call-update) | async-done | bytes 552976 | tf_op jit(solution)/shard_map/reduce_scatter | solution.py:133
  164.9 2.4 fusion.22
  167.5 14.5 %all-gather = s32[1,384,4]{2,1,0:T(8,128)S(1)} all-gather(s32[1,96,4]{2,1,0:T(8,128)S(1)} %copy.60), channel_id=2, replica_groups=mesh['dp'=4,'expert'=8] {'dp'}, dimensions={1}, use_global_device_ids=true | all-gather | bytes 7680 | tf_op jit(solution)/shard_map/all_gather | solution.py:153
  182.0 0.1 eq.94
  182.2 0.1 reshape.421
  182.3 2.3 reduce-window.19
  184.6 0.3 slice_reduce_fusion
  184.9 0.2 reduce-window.24
  185.1 0.2 mul.226
  185.4 6.2 scatter_custom_fusion
  191.7 23.9 %all-gather.8.cloned.1.call-done = bf16[384,2880]{0,1:T(8,128)(2,1)} async-done(((bf16[384,720]{0,1:T(8,128)(2,1)}), bf16[384,2880]{0,1:T(8,128)(2,1)}) %all-gather.8.cloned.1.call-update) | async-done | bytes 2211856 | tf_op jit(solution)/shard_map/all_gather | solution.py:147
  215.5 2.2 fusion.3
  217.7 2.2 fusion.5
  219.9 2.6 copy.76
  222.5 1.8 concatenate.31.clone
  224.3 12.0 %gather_fusion = bf16[2048,2880]{1,0:T(8,128)(2,1)} fusion(bf16[385,2880]{1,0:T(8,128)(2,1)S(1)} %concatenate.31.clone, s32[2048]{0:T(1024)S(1)} %fusion.67), kind=kCustom, calls=%fused_computation | custom fusion | bytes 23601152 | tf_op jit(solution)/shard_map/jit(_take)/gather | solution.py:164
  236.3 15.2 %copy.62 = bf16[8,256,2880]{1,2,0:T(8,128)(2,1)} copy(bf16[8,256,2880]{2,1,0:T(8,128)(2,1)} %bitcast.123) | data formatting | bytes 23592960 | tf_op jit(solution)/shard_map/jit(_take)/gather | solution.py:164
  251.5 6.5 broadcast_select_fusion
  258.0 134.2 %all_to_all.10 = bf16[8,256,2880]{1,2,0:T(8,128)(2,1)} all-to-all(bf16[8,256,2880]{1,2,0:T(8,128)(2,1)S(1)} %broadcast_select_fusion), channel_id=1, replica_groups=mesh['dp'=4,'expert'=8] {'expert'}, dimensions={0} | all-to-all | bytes 23592960 | tf_op jit(solution)/shard_map/all_to_all | solution.py:168
  392.2 16.3 %copy.63 = bf16[8,256,2880]{2,1,0:T(8,128)(2,1)} copy(bf16[8,256,2880]{1,2,0:T(8,128)(2,1)} %all_to_all.10) | data formatting | bytes 23592960 | tf_op jit(solution)/shard_map/all_to_all | solution.py:168
  408.4 15.1 %fusion.7 = f32[2048,720]{0,1:T(8,128)} fusion(bf16[2048,2880]{1,0:T(8,128)(2,1)} %bitcast.125, bf16[1,2880,720]{1,2,0:T(8,128)(2,1)} %param.34), kind=kOutput, calls=%fused_computation.22 | convolution fusion | flops 8493465600 | bytes 21841920 | tf_op jit(solution)/shard_map/dot_general | solution.py:171
  423.6 26.6 %convolution_convert_fusion = bf16[2048,2880]{0,1:T(8,128)(2,1)} fusion(bf16[1,720,2880]{2,1,0:T(8,128)(2,1)} %param.35, f32[2048,720]{0,1:T(8,128)} %fusion.7, bf16[2048,2880]{1,0:T(8,128)(2,1)} %bitcast.126, bf16[1,2880,720]{1,2,0:T(8,128)(2,1)} %param.33), kind=kOutput, calls=%fused_computation.7 | convolution fusion | flops 17004625920 | bytes 37785600 | tf_op jit(solution)/shard_map/dot_general | solution.py:176
  450.2 10.1 %copy.82 = bf16[360,8,8,256]{3,2,0,1:T(8,128)(2,1)} copy(bf16[360,8,8,256]{3,2,1,0:T(8,128)(2,1)} %bitcast.127) | data formatting | bytes 23592960 | tf_op jit(solution)/shard_map/reshape | solution.py:178
  460.3 5.5 all-to-all-start.1
  465.8 0.2 reduce_sum.69
  466.1 0.1 copy.66
  466.2 13.8 %all-gather.1 = bf16[1,384,4]{2,0,1:T(2,128)(2,1)S(1)} all-gather(bf16[1,96,4]{2,0,1:T(2,128)(2,1)S(1)} %copy.66), channel_id=3, replica_groups=mesh['dp'=4,'expert'=8] {'dp'}, dimensions={1}, use_global_device_ids=true | all-gather | bytes 3840 | tf_op jit(solution)/shard_map/all_gather | solution.py:154
  480.1 0.1 copy.75
  480.4 116.0 %all-to-all-done.1 = bf16[8,256,2880]{1,2,0:T(8,128)(2,1)} async-done(((bf16[8,256,2880]{1,2,0:T(8,128)(2,1)}), bf16[8,256,2880]{1,2,0:T(8,128)(2,1)}, u32[]{:S(2)}, u32[]{:S(2)}) %all-to-all-start.1) | async-done | bytes 11796512 | tf_op jit(solution)/shard_map/all_to_all | solution.py:180
  596.4 16.3 %copy.65 = bf16[8,256,2880]{2,1,0:T(8,128)(2,1)} copy(bf16[8,256,2880]{1,2,0:T(8,128)(2,1)} %all-to-all-done.1) | data formatting | bytes 23592960 | tf_op jit(solution)/shard_map/all_to_all | solution.py:180
  612.6 22.9 %gather_fusion.1 = bf16[1536,2880]{1,0:T(8,128)(2,1)} fusion(bf16[2048,2880]{1,0:T(8,128)(2,1)} %bitcast.122, s32[2048]{0:T(1024)S(1)} %pad_clamp_fusion), kind=kCustom, calls=%fused_computation.1 | custom fusion | bytes 17700864 | tf_op jit(solution)/shard_map/jit(_take)/gather | solution.py:181
  635.5 12.9 %gather.19 = bf16[384,4,2880]{2,1,0:T(4,128)(2,1)} reshape(bf16[1536,2880]{1,0:T(8,128)(2,1)} %gather_fusion.1) | data formatting | bytes 17694720 | tf_op jit(solution)/shard_map/jit(_take)/gather | solution.py:181
  648.4 20.9 %multiply_reduce_fusion = bf16[384,2880]{1,0:T(8,128)(2,1)S(1)} fusion(f32[384,4]{1,0:T(8,128)S(1)} %copy.75, bf16[384,4,2880]{2,1,0:T(4,128)(2,1)} %gather.19, pred[384,4]{1,0:T(8,128)(4,1)S(1)} %compare_and_fusion), kind=kLoop, calls=%fused_computation.4 | loop fusion | flops 16588800 | bytes 11066880
  669.4 2.5 copy.74
  672.1 43.0 %reduce-scatter.5.cloned.1.call-done = bf16[384,720]{0,1:T(8,128)(2,1)} async-done(((bf16[384,2880]{0,1:T(8,128)(2,1)}), bf16[384,720]{0,1:T(8,128)(2,1)}) %reduce-scatter.5.cloned.1.call-update) | async-done | bytes 552976 | tf_op jit(solution)/shard_map/reduce_scatter | solution.py:185
  715.1 2.1 add_convert_fusion
  717.3 1.3 copy.68
  718.6 0.6 gather_fusion.2
  719.2 40.3 %all-gather.2 = bf16[32,4,720]{2,1,0:T(4,128)(2,1)S(1)} all-gather(bf16[1,4,720]{2,1,0:T(4,128)(2,1)S(1)} %select_bitcast_fusion), channel_id=1, replica_groups=mesh['dp'=4,'expert'=8] {'dp','expert'}, dimensions={0}, use_global_device_ids=true | all-gather | bytes 190080 | tf_op jit(solution)/shard_map/all_gather | solution.py:194
  759.6 0.2 multiply_reduce_fusion.1
  759.8 1.0 copy.83
  760.8 1.2 reshape.426
  762.1 4.4 fusion.36
  (69 shorter events, 1.9 us)
Async XLA Ops:
  7.2 76.5 %copy-start = (bf16[512,2880]{0,1:T(8,128)(2,1)S(1)}, bf16[512,2880]{0,1:T(8,128)(2,1)}, u32[]{:S(2)}) copy-start(bf16[512,2880]{0,1:T(8,128)(2,1)} %param.27) | copy-start | bytes 8847364
  7.2 53.2 %all-gather.6.cloned.1.call-start = ((), (), s32[]{:S(2)}) async-start(), calls=%async_computation.4 | async-start | bytes 2764800 | tf_op jit(solution)/shard_map/all_gather | solution.py:101
  7.9 108.9 %all-reduce.3.cloned.1.call-start = ((), (), s32[]{:S(2)}) async-start(), calls=%async_computation.6 | async-start | bytes 196608 | tf_op jit(solution)/shard_map/psum | solution.py:136
  8.8 59.8 %copy-start.6 = (s32[384]{0:T(512)}, s32[384]{0:T(512)S(1)}, u32[]{:S(2)}) copy-start(s32[384]{0:T(512)S(1)} %reduce.7) | copy-start | bytes 4612
  62.6 6.0 copy-start.11
  62.6 6.0 copy-start.12
  79.6 3.0 copy-start.5
  81.9 0.8 copy-start.4
  83.6 81.3 %copy-start.3 = (bf16[384,720]{0,1:T(8,128)(2,1)S(1)}, bf16[384,720]{0,1:T(8,128)(2,1)}, u32[]{:S(2)}) copy-start(bf16[384,720]{0,1:T(8,128)(2,1)} %param.19) | copy-start | bytes 1658884
  83.6 81.3 %reduce-scatter.3.cloned.1.call-start = ((), (), s32[]{:S(2)}) async-start(), calls=%async_computation.5 | async-start | bytes 2764800 | tf_op jit(solution)/shard_map/reduce_scatter | solution.py:133
  87.8 79.6 %copy-start.9 = (s32[1,96,4]{1,2,0:T(4,128)S(1)}, s32[1,96,4]{1,2,0:T(4,128)}, u32[]{:S(2)}) copy-start(s32[1,96,4]{1,2,0:T(4,128)} %param.22) | copy-start | bytes 4612
  87.8 129.9 %copy-start.8 = (f32[2880]{0:T(1024)S(1)}, f32[2880]{0:T(1024)}, u32[]{:S(2)}) copy-start(f32[2880]{0:T(1024)} %param.32) | copy-start | bytes 34564
  87.8 127.7 %all-gather.8.cloned.1.call-start = ((), (), s32[]{:S(2)}) async-start(), calls=%async_computation.7 | async-start | bytes 2764800 | tf_op jit(solution)/shard_map/all_gather | solution.py:147
  460.3 5.7 copy-start.10
  460.3 136.1 %all-to-all-start.1 = ((bf16[8,256,2880]{1,2,0:T(8,128)(2,1)}), bf16[8,256,2880]{1,2,0:T(8,128)(2,1)}, u32[]{:S(2)}, u32[]{:S(2)}) async-start(bf16[8,256,2880]{1,2,0:T(8,128)(2,1)} %bitcast.124), calls=%async_computation.2 | async-start | bytes 23592960 | tf_op jit(solution)/shard_map/all_to_all | solution.py:180
  465.8 249.3 %reduce-scatter.5.cloned.1.call-start = ((), (), s32[]{:S(2)}) async-start(), calls=%async_computation.8 | async-start | bytes 2764800 | tf_op jit(solution)/shard_map/reduce_scatter | solution.py:185
  669.3 2.6 copy-start.7
  669.3 45.8 %copy-start.2 = (bf16[384,720]{0,1:T(8,128)(2,1)S(1)}, bf16[384,720]{0,1:T(8,128)(2,1)}, u32[]{:S(2)}) copy-start(bf16[384,720]{0,1:T(8,128)(2,1)} %fusion.22) | copy-start | bytes 1658884
  715.1 51.4 %copy-start.1 = (bf16[512,2880]{0,1:T(8,128)(2,1)S(1)}, bf16[512,2880]{0,1:T(8,128)(2,1)}, u32[]{:S(2)}) copy-start(bf16[512,2880]{0,1:T(8,128)(2,1)} %param.27) | copy-start | bytes 8847364
Sparse Core Ops, SparseCore 0:
  9.6 50.7 all-gather.5
  83.7 33.0 all-reduce.2
  119.3 45.5 reduce-scatter.2
  167.5 47.9 all-gather.7
  672.0 43.0 reduce-scatter.4
where the time goes:
time: 775 us; the launch traced here: 773 us
  waiting for transfers between devices  309 us (40%)
  blocking collectives  203 us (26%)
  local copies, waits for them, and re-layouts  131 us (17%)
  matrix products  67.9 us (9%)
  other arithmetic  43.1 us (6%)
  between operations  14.1 us (2%)
    all_to_all x1, blocking collectives, shards(): lax.all_to_all(outgoing, 'expert', split_axis=0, concat_axis=0, tiled=True)  134 us
    all_to_all x1, waiting for transfers between devices, shards(): lax.all_to_all(shares_out, 'expert', split_axis=0, concat_axis=0, tiled=T...  116 us
    all_gather x1, waiting for transfers between devices, shards(): gathered_rows = lax.all_gather(hidden, 'dp', axis=1, tiled=True)  48.1 us
    reduce_scatter x1, waiting for transfers between devices, shards(): lax.psum_scatter(partial_out.astype(jnp.bfloat16), 'dp', scatter_dimensio...  48 us
    reduce_scatter x1, waiting for transfers between devices, shards(): lax.psum_scatter(mixture.astype(jnp.bfloat16), 'dp', scatter_dimension=1,...  43 us
    all_gather x1, blocking collectives, shards(): spread_rows = lax.all_gather(chosen, ('dp', 'expert'), axis=0, tiled=True)  40.3 us
    gather x2, local copies, waits for them, and re-layouts, shards(): jnp.take(answers.reshape(experts * col_capacity, width), target, axis=0)  35.8 us
    psum x1, waiting for transfers between devices, shards(): lax.psum(jnp.dot(blended_hidden, output_down_maps, preferred_element_type...  29 us
  transfers between devices with their start and end apart: 6, of which 6 were waited for; matrix products, arithmetic and copies ran while one was open for 2% of the time, Pallas kernels for 0%

commit v1 on v0

--- a/solution.py
+++ b/solution.py
@@ -133,11 +133,14 @@
     mine_out = lax.psum_scatter(
         partial_out.astype(jnp.bfloat16), "dp", scatter_dimension=1, tiled=True
     ).astype(jnp.float32)
-    output_reduced = lax.psum(
-        jnp.dot(blended_hidden, output_down_maps, preferred_element_type=jnp.float32).astype(
-            jnp.bfloat16
+    output_reduced = jnp.sum(
+        lax.all_gather(
+            jnp.dot(blended_hidden, output_down_maps, preferred_element_type=jnp.float32).astype(
+                jnp.bfloat16
+            ),
+            "dp",
         ),
-        "dp",
+        axis=0,
     )
     selected_output = jnp.where(adapter_mask, output_reduced, jnp.zeros_like(output_reduced))
     adapter_delta = adapter_scale * jnp.dot(

time: 775 us -> 745 us (0.961)
  waiting for transfers between devices: 309 us -> 262 us
  blocking collectives: 203 us -> 220 us
    psum x1 -> x0, waiting for transfers between devices: 29 us -> none  [shards(): lax.psum(jnp.dot(blended_hidden, output_down_maps, preferred_element_type...]
    reduce_scatter x1, waiting for transfers between devices: 48 us -> 29.5 us  [shards(): lax.psum_scatter(partial_out.astype(jnp.bfloat16), 'dp', scatter_dimensio...]
    all_gather x0 -> x1, blocking collectives: none -> 17.7 us  [shards(): lax.all_gather(jnp.dot(blended_hidden, output_down_maps, preferred_elemen...]
  transfers between devices with their start and end apart: 6 -> 5, of which waited for: 6 -> 5; matrix products, arithmetic and copies ran while one was open for 2% -> 2% of each run, Pallas kernels for 0% -> 0%
where the time goes in v1:
time: 745 us; the launch traced here: 743 us
  waiting for transfers between devices  262 us (35%)
  blocking collectives  220 us (30%)
  local copies, waits for them, and re-layouts  131 us (18%)
  matrix products  67.2 us (9%)
  other arithmetic  43.2 us (6%)
  between operations  14.1 us (2%)
    all_to_all x1, blocking collectives, shards(): lax.all_to_all(outgoing, 'expert', split_axis=0, concat_axis=0, tiled=True)  134 us
    all_to_all x1, waiting for transfers between devices, shards(): lax.all_to_all(shares_out, 'expert', split_axis=0, concat_axis=0, tiled=T...  116 us
    all_gather x1, waiting for transfers between devices, shards(): gathered_rows = lax.all_gather(hidden, 'dp', axis=1, tiled=True)  48.1 us
    reduce_scatter x1, waiting for transfers between devices, shards(): lax.psum_scatter(mixture.astype(jnp.bfloat16), 'dp', scatter_dimension=1,...  43 us
    all_gather x1, blocking collectives, shards(): spread_rows = lax.all_gather(chosen, ('dp', 'expert'), axis=0, tiled=True)  40.3 us
    gather x2, local copies, waits for them, and re-layouts, shards(): jnp.take(answers.reshape(experts * col_capacity, width), target, axis=0)  35.8 us
    reduce_scatter x1, waiting for transfers between devices, shards(): lax.psum_scatter(partial_out.astype(jnp.bfloat16), 'dp', scatter_dimensio...  29.5 us
    gather x2, local copies, waits for them, and re-layouts, shards(): jnp.take(padded, table, axis=0).reshape(experts, col_capacity, width)  27.2 us
  transfers between devices with their start and end apart: 5, of which 5 were waited for; matrix products, arithmetic and copies ran while one was open for 2% of the time, Pallas kernels for 0%

profile of v1, /device:TPU:0, one launch (start us, length us, event | category | flops | bytes accessed | tf_op | source)
XLA Modules:
  0.0 743.1 jit_solution(6430327750168231012)
XLA Ops:
  7.2 0.7 all-gather.7.cloned.1.call-update
  8.0 0.8 reduce.8
  8.8 0.8 compare_reduce_fusion
  9.7 0.3 reduce-window.15
  10.1 0.7 exp.18
  10.9 0.9 select_reduce_fusion
  11.9 0.3 multiply_cosine_fusion
  12.3 48.1 %all-gather.7.cloned.1.call-done = bf16[384,2880]{0,1:T(8,128)(2,1)} async-done(((bf16[384,720]{0,1:T(8,128)(2,1)}), bf16[384,2880]{0,1:T(8,128)(2,1)}) %all-gather.7.cloned.1.call-update) | async-done | bytes 2211856 | tf_op jit(solution)/shard_map/all_gather | solution.py:101
  60.4 2.2 fusion
  62.6 5.9 fusion.14
  68.5 4.8 fusion.21
  73.3 2.5 copy.58
  75.8 1.2 slice_bitcast_fusion
  77.0 0.9 slice_bitcast_fusion.1
  77.9 0.3 fusion.63
  78.3 1.3 fusion.13
  79.6 2.2 fusion.23
  81.8 0.7 copy-done.4
  82.6 3.1 convolution_convert_fusion.1
  85.8 1.3 convolution_convert_fusion.2
  87.1 17.7 %all-gather = bf16[1536,128]{1,0:T(8,128)(2,1)S(1)} all-gather(bf16[384,128]{1,0:T(8,128)(2,1)S(1)} %convolution_convert_fusion.2), channel_id=2, replica_groups=mesh['dp'=4,'expert'=8] {'dp'}, dimensions={0}, use_global_device_ids=true | all-gather | bytes 491520 | tf_op jit(solution)/shard_map/all_gather | solution.py:137
  104.8 29.5 %reduce-scatter.3.cloned.1.call-done = bf16[384,720]{0,1:T(8,128)(2,1)} async-done(((bf16[384,2880]{0,1:T(8,128)(2,1)}), bf16[384,720]{0,1:T(8,128)(2,1)}) %reduce-scatter.3.cloned.1.call-update) | async-done | bytes 552976 | tf_op jit(solution)/shard_map/reduce_scatter | solution.py:133
  134.3 2.4 fusion.22
  136.9 14.3 %all-gather.1 = s32[1,384,4]{2,1,0:T(8,128)S(1)} all-gather(s32[1,96,4]{2,1,0:T(8,128)S(1)} %copy.60), channel_id=3, replica_groups=mesh['dp'=4,'expert'=8] {'dp'}, dimensions={1}, use_global_device_ids=true | all-gather | bytes 7680 | tf_op jit(solution)/shard_map/all_gather | solution.py:156
  151.2 0.1 eq.94
  151.3 0.1 reshape.421
  151.5 2.3 reduce-window.19
  153.7 0.3 slice_reduce_fusion
  154.0 0.2 reduce-window.24
  154.2 0.2 mul.226
  154.5 6.2 scatter_custom_fusion
  160.8 24.9 %all-gather.9.cloned.1.call-done = bf16[384,2880]{0,1:T(8,128)(2,1)} async-done(((bf16[384,720]{0,1:T(8,128)(2,1)}), bf16[384,2880]{0,1:T(8,128)(2,1)}) %all-gather.9.cloned.1.call-update) | async-done | bytes 2211856 | tf_op jit(solution)/shard_map/all_gather | solution.py:150
  185.6 2.2 fusion.3
  187.8 2.2 fusion.5
  190.0 2.6 copy.76
  192.6 1.8 concatenate.31.clone
  194.4 12.0 %gather_fusion = bf16[2048,2880]{1,0:T(8,128)(2,1)} fusion(bf16[385,2880]{1,0:T(8,128)(2,1)S(1)} %concatenate.31.clone, s32[2048]{0:T(1024)S(1)} %fusion.67), kind=kCustom, calls=%fused_computation | custom fusion | bytes 23601152 | tf_op jit(solution)/shard_map/jit(_take)/gather | solution.py:167
  206.4 15.2 %copy.62 = bf16[8,256,2880]{1,2,0:T(8,128)(2,1)} copy(bf16[8,256,2880]{2,1,0:T(8,128)(2,1)} %bitcast.124) | data formatting | bytes 23592960 | tf_op jit(solution)/shard_map/jit(_take)/gather | solution.py:167
  221.6 6.5 broadcast_select_fusion
  228.1 134.2 %all_to_all.10 = bf16[8,256,2880]{1,2,0:T(8,128)(2,1)} all-to-all(bf16[8,256,2880]{1,2,0:T(8,128)(2,1)S(1)} %broadcast_select_fusion), channel_id=1, replica_groups=mesh['dp'=4,'expert'=8] {'expert'}, dimensions={0} | all-to-all | bytes 23592960 | tf_op jit(solution)/shard_map/all_to_all | solution.py:171
  362.3 16.3 %copy.63 = bf16[8,256,2880]{2,1,0:T(8,128)(2,1)} copy(bf16[8,256,2880]{1,2,0:T(8,128)(2,1)} %all_to_all.10) | data formatting | bytes 23592960 | tf_op jit(solution)/shard_map/all_to_all | solution.py:171
  378.6 15.1 %fusion.7 = f32[2048,720]{0,1:T(8,128)} fusion(bf16[2048,2880]{1,0:T(8,128)(2,1)} %bitcast.126, bf16[1,2880,720]{1,2,0:T(8,128)(2,1)} %param.34), kind=kOutput, calls=%fused_computation.22 | convolution fusion | flops 8493465600 | bytes 21841920 | tf_op jit(solution)/shard_map/dot_general | solution.py:174
  393.7 26.6 %convolution_convert_fusion = bf16[2048,2880]{0,1:T(8,128)(2,1)} fusion(bf16[1,720,2880]{2,1,0:T(8,128)(2,1)} %param.35, f32[2048,720]{0,1:T(8,128)} %fusion.7, bf16[2048,2880]{1,0:T(8,128)(2,1)} %bitcast.127, bf16[1,2880,720]{1,2,0:T(8,128)(2,1)} %param.33), kind=kOutput, calls=%fused_computation.7 | convolution fusion | flops 17004625920 | bytes 37785600 | tf_op jit(solution)/shard_map/dot_general | solution.py:179
  420.3 10.1 %copy.82 = bf16[360,8,8,256]{3,2,0,1:T(8,128)(2,1)} copy(bf16[360,8,8,256]{3,2,1,0:T(8,128)(2,1)} %bitcast.128) | data formatting | bytes 23592960 | tf_op jit(solution)/shard_map/reshape | solution.py:181
  430.4 5.5 all-to-all-start.1
  436.0 0.2 reduce_sum.82
  436.2 0.1 copy.66
  436.3 13.8 %all-gather.2 = bf16[1,384,4]{2,0,1:T(2,128)(2,1)S(1)} all-gather(bf16[1,96,4]{2,0,1:T(2,128)(2,1)S(1)} %copy.66), channel_id=4, replica_groups=mesh['dp'=4,'expert'=8] {'dp'}, dimensions={1}, use_global_device_ids=true | all-gather | bytes 3840 | tf_op jit(solution)/shard_map/all_gather | solution.py:157
  450.3 0.1 copy.75
  450.5 116.0 %all-to-all-done.1 = bf16[8,256,2880]{1,2,0:T(8,128)(2,1)} async-done(((bf16[8,256,2880]{1,2,0:T(8,128)(2,1)}), bf16[8,256,2880]{1,2,0:T(8,128)(2,1)}, u32[]{:S(2)}, u32[]{:S(2)}) %all-to-all-start.1) | async-done | bytes 11796512 | tf_op jit(solution)/shard_map/all_to_all | solution.py:183
  566.5 16.3 %copy.65 = bf16[8,256,2880]{2,1,0:T(8,128)(2,1)} copy(bf16[8,256,2880]{1,2,0:T(8,128)(2,1)} %all-to-all-done.1) | data formatting | bytes 23592960 | tf_op jit(solution)/shard_map/all_to_all | solution.py:183
  582.7 22.9 %gather_fusion.1 = bf16[1536,2880]{1,0:T(8,128)(2,1)} fusion(bf16[2048,2880]{1,0:T(8,128)(2,1)} %bitcast.123, s32[2048]{0:T(1024)S(1)} %pad_clamp_fusion), kind=kCustom, calls=%fused_computation.1 | custom fusion | bytes 17700864 | tf_op jit(solution)/shard_map/jit(_take)/gather | solution.py:184
  605.6 12.9 %gather.19 = bf16[384,4,2880]{2,1,0:T(4,128)(2,1)} reshape(bf16[1536,2880]{1,0:T(8,128)(2,1)} %gather_fusion.1) | data formatting | bytes 17694720 | tf_op jit(solution)/shard_map/jit(_take)/gather | solution.py:184
  618.5 20.9 %multiply_reduce_fusion = bf16[384,2880]{1,0:T(8,128)(2,1)S(1)} fusion(f32[384,4]{1,0:T(8,128)S(1)} %copy.75, bf16[384,4,2880]{2,1,0:T(4,128)(2,1)} %gather.19, pred[384,4]{1,0:T(8,128)(4,1)S(1)} %compare_and_fusion), kind=kLoop, calls=%fused_computation.4 | loop fusion | flops 16588800 | bytes 11066880
  639.5 2.5 copy.74
  642.2 43.0 %reduce-scatter.5.cloned.1.call-done = bf16[384,720]{0,1:T(8,128)(2,1)} async-done(((bf16[384,2880]{0,1:T(8,128)(2,1)}), bf16[384,720]{0,1:T(8,128)(2,1)}) %reduce-scatter.5.cloned.1.call-update) | async-done | bytes 552976 | tf_op jit(solution)/shard_map/reduce_scatter | solution.py:188
  685.2 2.1 add_convert_fusion
  687.3 1.3 copy.68
  688.6 0.6 gather_fusion.2
  689.3 40.3 %all-gather.3 = bf16[32,4,720]{2,1,0:T(4,128)(2,1)S(1)} all-gather(bf16[1,4,720]{2,1,0:T(4,128)(2,1)S(1)} %select_bitcast_fusion), channel_id=1, replica_groups=mesh['dp'=4,'expert'=8] {'dp','expert'}, dimensions={0}, use_global_device_ids=true | all-gather | bytes 190080 | tf_op jit(solution)/shard_map/all_gather | solution.py:197
  729.7 0.2 multiply_reduce_fusion.1
  729.9 1.0 copy.83
  730.8 1.2 reshape.426
  732.2 4.4 fusion.36
  (66 shorter events, 1.9 us)
Async XLA Ops:
  7.2 75.4 %copy-start = (bf16[512,2880]{0,1:T(8,128)(2,1)S(1)}, bf16[512,2880]{0,1:T(8,128)(2,1)}, u32[]{:S(2)}) copy-start(bf16[512,2880]{0,1:T(8,128)(2,1)} %param.27) | copy-start | bytes 8847364
  7.2 53.2 %all-gather.7.cloned.1.call-start = ((), (), s32[]{:S(2)}) async-start(), calls=%async_computation.4 | async-start | bytes 2764800 | tf_op jit(solution)/shard_map/all_gather | solution.py:101
  7.9 126.4 %reduce-scatter.3.cloned.1.call-start = ((), (), s32[]{:S(2)}) async-start(), calls=%async_computation.5 | async-start | bytes 2764800 | tf_op jit(solution)/shard_map/reduce_scatter | solution.py:133
  8.8 59.8 %copy-start.5 = (s32[384]{0:T(512)}, s32[384]{0:T(512)S(1)}, u32[]{:S(2)}) copy-start(s32[384]{0:T(512)S(1)} %reduce.8) | copy-start | bytes 4612
  62.6 6.0 copy-start.10
  62.6 6.0 copy-start.11
  81.8 0.8 copy-start.4
  82.6 51.7 %copy-start.3 = (bf16[384,720]{0,1:T(8,128)(2,1)S(1)}, bf16[384,720]{0,1:T(8,128)(2,1)}, u32[]{:S(2)}) copy-start(bf16[384,720]{0,1:T(8,128)(2,1)} %param.19) | copy-start | bytes 1658884
  85.7 51.1 %copy-start.8 = (s32[1,96,4]{1,2,0:T(4,128)S(1)}, s32[1,96,4]{1,2,0:T(4,128)}, u32[]{:S(2)}) copy-start(s32[1,96,4]{1,2,0:T(4,128)} %param.22) | copy-start | bytes 4612
  85.7 102.1 %copy-start.7 = (f32[2880]{0:T(1024)S(1)}, f32[2880]{0:T(1024)}, u32[]{:S(2)}) copy-start(f32[2880]{0:T(1024)} %param.32) | copy-start | bytes 34564
  85.7 99.9 %all-gather.9.cloned.1.call-start = ((), (), s32[]{:S(2)}) async-start(), calls=%async_computation.6 | async-start | bytes 2764800 | tf_op jit(solution)/shard_map/all_gather | solution.py:150
  430.4 5.7 copy-start.9
  430.4 136.1 %all-to-all-start.1 = ((bf16[8,256,2880]{1,2,0:T(8,128)(2,1)}), bf16[8,256,2880]{1,2,0:T(8,128)(2,1)}, u32[]{:S(2)}, u32[]{:S(2)}) async-start(bf16[8,256,2880]{1,2,0:T(8,128)(2,1)} %bitcast.125), calls=%async_computation.2 | async-start | bytes 23592960 | tf_op jit(solution)/shard_map/all_to_all | solution.py:183
  435.9 249.3 %reduce-scatter.5.cloned.1.call-start = ((), (), s32[]{:S(2)}) async-start(), calls=%async_computation.7 | async-start | bytes 2764800 | tf_op jit(solution)/shard_map/reduce_scatter | solution.py:188
  639.4 2.6 copy-start.6
  639.5 45.7 %copy-start.2 = (bf16[384,720]{0,1:T(8,128)(2,1)S(1)}, bf16[384,720]{0,1:T(8,128)(2,1)}, u32[]{:S(2)}) copy-start(bf16[384,720]{0,1:T(8,128)(2,1)} %fusion.22) | copy-start | bytes 1658884
  685.2 51.4 %copy-start.1 = (bf16[512,2880]{0,1:T(8,128)(2,1)S(1)}, bf16[512,2880]{0,1:T(8,128)(2,1)}, u32[]{:S(2)}) copy-start(bf16[512,2880]{0,1:T(8,128)(2,1)} %param.27) | copy-start | bytes 8847364
Sparse Core Ops, SparseCore 0:
  9.6 50.7 all-gather.6
  85.8 48.4 reduce-scatter.2
  136.9 48.7 all-gather.8
  642.1 42.9 reduce-scatter.4
